TPU v7x, 512 devices: a whole 4x8x8 slice. The times are simulated.
512 devices in a mesh: tm: 16 (over y, core), pre: 32 (over z, x).
Axes of the slice: x: 4, y: 8, z: 8, core: 2. Of those that a mesh axis runs over, the one named last changes fastest.
Arguments:
- spikes: int32 [3072, 16384], P('tm', 'pre'), may hold values from 0 to 1
- trace_decay: float32 [16384], P('pre'), may hold values from 0.96 to 1
- pseudo_deriv: bfloat16 [3072, 16384], P('pre', 'tm'), may hold values from 0 to 0.29882812
- readout_weight: bfloat16 [16384, 512], P('pre'), may hold values from -2 to 2
- feedback_weight: bfloat16 [16384, 512], P('tm'), may hold values from -6 to 6
- targets: int32 [3072], P('tm'), may hold values from 0 to 511
Outputs:
- gradient: float32 [16384, 16384], P('pre', 'tm')
All inputs are finite; a program needn't handle non-finite values.
Results may differ from a plain program's by a relative error of at most 0.0022.
Values may be sent and summed in bfloat16 or wider, within the bound.
No kernel may reach another device: no remote copies, remote signals or barrier semaphores. Data moves between devices by JAX's collectives and lax.ppermute only.
A program may use at most 64 MiB of HBM per device.

v0:
```python
import jax
import jax.numpy as jnp
from jax import lax
from jax.sharding import PartitionSpec as P


def prefix(value, axis, combine, identity):
    count, index = (lax.axis_size(axis), lax.axis_index(axis))
    everything = jax.tree.map(lambda part: lax.all_gather(part, axis), value)
    start = jax.tree.map(
        lambda part, zero: jnp.broadcast_to(jnp.asarray(zero, part.dtype), part.shape),
        value,
        identity,
    )

    def step(k, before):
        reached = k < index
        new = combine(before, jax.tree.map(lambda part: part[k], everything))
        return jax.tree.map(lambda a, b: jnp.where(reached, a, b), new, before)

    return lax.fori_loop(0, count, step, start)


def combine_pairs(earlier, later):
    return (earlier[0] * later[0], later[1] + later[0] * earlier[1])


def local_traces(spikes, decays):
    factor = jnp.broadcast_to(decays[None, :], spikes.shape)
    source = (1.0 - decays)[None, :] * spikes.astype(jnp.float32)
    return lax.associative_scan(combine_pairs, (factor, source), axis=0)


def error_rows(spikes, readout_weight, targets):
    partial_logits = jnp.dot(
        spikes.astype(jnp.bfloat16), readout_weight, preferred_element_type=jnp.float32
    )
    logits = lax.psum(partial_logits, "pre")
    class_prob = jax.nn.softmax(logits, axis=-1)
    classes = lax.broadcasted_iota(jnp.int32, logits.shape, 1)
    onehot = (targets[:, None] == classes).astype(jnp.float32)
    return (class_prob - onehot).astype(jnp.bfloat16)


def make_signal(errors_all, feedback_weight, derivs, offset):
    err_rows = lax.dynamic_slice_in_dim(errors_all, offset, derivs.shape[0], 0)
    signal = lax.dot_general(
        err_rows, feedback_weight, (((1,), (1,)), ((), ())), preferred_element_type=jnp.float32
    )
    return (signal * derivs.astype(jnp.float32)).astype(jnp.bfloat16)


def outer_sum(left_rows, right_rows):
    return lax.dot_general(
        left_rows, right_rows, (((0,), (0,)), ((), ())), preferred_element_type=jnp.float32
    )


def shards(spikes, trace_decay, pseudo_deriv, readout_weight, feedback_weight, targets):
    errors = error_rows(spikes, readout_weight, targets)
    errors_all = lax.all_gather(errors, "tm", axis=0, tiled=True)
    powers, states = local_traces(spikes, trace_decay)
    carried = prefix(
        (powers[-1], states[-1]),
        "tm",
        combine_pairs,
        (jnp.ones_like(trace_decay), jnp.zeros_like(trace_decay)),
    )
    incoming = carried[1]
    traces = (states + powers * incoming[None, :]).astype(jnp.bfloat16)
    offset = lax.axis_index("pre") * pseudo_deriv.shape[0]
    sources = make_signal(errors_all, feedback_weight, pseudo_deriv, offset)
    signal_all = lax.all_gather(sources, "pre", axis=0, tiled=True)
    return outer_sum(lax.all_gather(traces, "tm", axis=0, tiled=True), signal_all)


def solution(mesh):
    placed = (P("tm", "pre"), P("pre"), P("pre", "tm"), P("pre", None), P("tm", None), P("tm"))
    return jax.shard_map(
        shards, mesh=mesh, in_specs=placed, out_specs=P("pre", "tm"), check_vma=False
    )
```

profile of v0, /device:TPU:1, one launch (start us, length us, event | category | flops | bytes accessed | tf_op | source)
XLA Modules:
  0.0 374.8 jit_solution(8021454056844879361)
XLA Ops:
  6.5 0.0 copy-start
  6.5 0.0 copy-start.3
  6.5 0.0 all-reduce.30.cloned.1.call-start
  6.5 2.3 fusion.3
  8.8 0.0 all-reduce.30.cloned.1.call-update
  8.8 0.0 all-gather.8.cloned.1.call-start
  8.9 0.7 broadcast_subtract_fusion
  9.6 1.0 convert_multiply_fusion
  10.6 0.0 copy-start.1
  10.6 0.1 slice.194
  10.8 0.1 slice.192
  10.9 0.2 slice.190
  11.1 0.0 copy-done.3
  12.4 0.0 copy-done.1
  12.4 0.0 slice-start
  12.7 0.0 copy-start.4
  12.8 0.1 fusion.2
  12.9 0.2 slice-done
  13.2 0.1 pad.98
  13.3 0.0 copy-start.2
  13.3 0.1 pad.99
  13.3 20.9 %all-gather = f32[16,1,512]{2,1,0:T(1,128)S(1)} all-gather(f32[1,1,512]{2,1,0:T(1,128)S(1)} %add_bitcast_fusion.1), channel_id=1, replica_groups=mesh['tm'=16,'pre'=32] {'tm'}, dimensions={0}, use_global_device_ids=true | all-gather | bytes 34816 | tf_op jit(solution)/shard_map/all_gather | solution.py:9
  34.3 0.1 pad.113
  34.4 0.1 pad.112
  34.4 134.3 %all-reduce.30.cloned.1.call-done = f32[192,512]{1,0:T(8,128)} async-done(((f32[192,512]{1,0:T(8,128)}), f32[192,512]{1,0:T(8,128)}) %all-reduce.30.cloned.1.call-update) | async-done | bytes 393232 | tf_op jit(solution)/shard_map/psum | solution.py:38
  168.8 1.1 reduce_max.9
  169.9 1.2 fusion.1
  171.1 0.0 copy-done.4
  171.1 1.9 subtract_convert_fusion
  173.0 0.0 all-gather.8.cloned.1.call-update
  173.0 0.0 all-gather.6.cloned.1.call-start
  173.0 22.0 %all-gather.1 = f32[16,1,512]{2,1,0:T(1,128)S(1)} all-gather(f32[1,1,512]{2,1,0:T(1,128)S(1)} %add_bitcast_fusion), channel_id=1, replica_groups=mesh['tm'=16,'pre'=32] {'tm'}, dimensions={0}, use_global_device_ids=true | all-gather | bytes 34816 | tf_op jit(solution)/shard_map/all_gather | solution.py:9
  195.0 0.9 while.14
  195.9 0.8 add_convert_fusion
  196.8 0.0 all-gather.6.cloned.1.call-update
  196.8 0.0 all-gather.10.cloned.1.call-start
  196.9 21.5 %all-gather.8.cloned.1.call-done = bf16[3072,512]{1,0:T(8,128)(2,1)} async-done(((bf16[192,512]{1,0:T(8,128)(2,1)}), bf16[3072,512]{1,0:T(8,128)(2,1)}) %all-gather.8.cloned.1.call-update) | async-done | bytes 3145744 | tf_op jit(solution)/shard_map/all_gather | solution.py:61
  218.4 0.0 copy-done
  218.4 0.0 copy-done.2
  218.4 2.0 fusion
  220.4 0.0 all-gather.10.cloned.1.call-update
  220.4 42.9 %all-gather.6.cloned.1.call-done = bf16[3072,512]{1,0:T(8,128)(2,1)} async-done(((bf16[192,512]{1,0:T(8,128)(2,1)}), bf16[3072,512]{1,0:T(8,128)(2,1)}) %all-gather.6.cloned.1.call-update) | async-done | bytes 3145744 | tf_op jit(solution)/shard_map/all_gather | solution.py:74
  263.4 96.4 %all-gather.10.cloned.1.call-done = bf16[3072,1024]{1,0:T(8,128)(2,1)} async-done(((bf16[96,1024]{1,0:T(8,128)(2,1)}), bf16[3072,1024]{1,0:T(8,128)(2,1)}) %all-gather.10.cloned.1.call-update) | async-done | bytes 6291472 | tf_op jit(solution)/shard_map/all_gather | solution.py:73
  359.8 8.5 %fusion.19 = f32[512,1024]{1,0:T(8,128)} fusion(bf16[3072,512]{1,0:T(8,128)(2,1)} %all-gather.6.cloned.1.call-done, bf16[3072,1024]{1,0:T(8,128)(2,1)} %all-gather.10.cloned.1.call-done), kind=kOutput, calls=%fused_computation.73 | convolution fusion | flops 3221225472 | bytes 11534336 | tf_op jit(solution)/shard_map/dot_general | solution.py:54
  (116 shorter events, 1.6 us)
Async XLA Ops:
  6.5 211.8 %copy-start = (bf16[1024,512]{1,0:T(8,128)(2,1)S(1)}, bf16[1024,512]{1,0:T(8,128)(2,1)}, u32[]{:S(2)}) copy-start(bf16[1024,512]{1,0:T(8,128)(2,1)} %param.12) | copy-start | bytes 3145732
  6.5 4.6 %copy-start.3 = (f32[512]{0:T(512)S(1)}, f32[512]{0:T(512)}, u32[]{:S(2)}) copy-start(f32[512]{0:T(512)} %param.9) | copy-start | bytes 6148
  6.5 162.2 %all-reduce.30.cloned.1.call-start = ((), (), s32[]{:S(2)}) async-start(), calls=%async_computation.1 | async-start | bytes 786432 | tf_op jit(solution)/shard_map/psum | solution.py:38
  8.8 209.5 %all-gather.8.cloned.1.call-start = ((), (), s32[]{:S(2)}) async-start(), calls=%async_computation.2 | async-start | bytes 3342336 | tf_op jit(solution)/shard_map/all_gather | solution.py:61
  10.6 1.7 copy-start.1
  12.4 0.7 slice-start
  12.7 158.4 %copy-start.4 = (s32[192]{0:T(256)S(1)}, s32[192]{0:T(256)}, u32[]{:S(2)}) copy-start(s32[192]{0:T(256)} %param.13) | copy-start | bytes 2308
  13.3 205.1 %copy-start.2 = (bf16[96,1024]{1,0:T(8,128)(2,1)S(1)}, bf16[96,1024]{1,0:T(8,128)(2,1)}, u32[]{:S(2)}) copy-start(bf16[96,1024]{1,0:T(8,128)(2,1)} %param.10) | copy-start | bytes 589828
  173.0 90.4 %all-gather.6.cloned.1.call-start = ((), (), s32[]{:S(2)}) async-start(), calls=%async_computation | async-start | bytes 3342336 | tf_op jit(solution)/shard_map/all_gather | solution.py:74
  196.8 163.0 %all-gather.10.cloned.1.call-start = ((), (), s32[]{:S(2)}) async-start(), calls=%async_computation.3 | async-start | bytes 6488064 | tf_op jit(solution)/shard_map/all_gather | solution.py:73
Sparse Core Ops, SparseCore 0:
  10.8 157.9 all-reduce.29
  173.1 45.2 all-gather.7
  220.7 42.6 all-gather.5
  266.9 92.9 all-gather.9
where the time goes:
time: 375 us
  waiting for transfers between devices  295 us (79%)
  blocking collectives  42.9 us (11%)
  between operations  13.8 us (4%)
  matrix products  12.8 us (3%)
  other arithmetic  7.6 us (2%)
    psum x1, waiting for transfers between devices, error_rows(): logits = lax.psum(partial_logits, 'pre')  134 us
    all_gather x1, waiting for transfers between devices, shards(): signal_all = lax.all_gather(sources, 'pre', axis=0, tiled=True)  96.4 us
    all_gather x1, waiting for transfers between devices, shards(): lax.all_gather(traces, 'tm', axis=0, tiled=True)  42.9 us
    all_gather x2, blocking collectives, prefix(): everything = jax.tree.map(lambda part: lax.all_gather(part, axis), value)  42.9 us
    all_gather x1, waiting for transfers between devices, shards(): errors_all = lax.all_gather(errors, 'tm', axis=0, tiled=True)  21.5 us
    dot_general x1, matrix products, outer_sum(): lax.dot_general(left_rows, right_rows, (((0,), (0,)), ((), ())), preferre...  8.49 us
  transfers between devices with their start and end apart: 4, of which 4 were waited for; matrix products, arithmetic and copies ran while one was open for 2% of the time, Pallas kernels for 0%

commit v1 on v0

--- a/solution.py
+++ b/solution.py
@@ -35,7 +35,7 @@
     partial_logits = jnp.dot(
         spikes.astype(jnp.bfloat16), readout_weight, preferred_element_type=jnp.float32
     )
-    logits = lax.psum(partial_logits, "pre")
+    logits = jnp.sum(lax.all_gather(partial_logits, "pre"), axis=0)
     class_prob = jax.nn.softmax(logits, axis=-1)
     classes = lax.broadcasted_iota(jnp.int32, logits.shape, 1)
     onehot = (targets[:, None] == classes).astype(jnp.float32)

time: 375 us -> 346 us (0.923)
  waiting for transfers between devices: 295 us -> 267 us
  blocking collectives: 42.9 us -> 38.9 us
    psum x1 -> x0, waiting for transfers between devices: 134 us -> none  [error_rows(): logits = lax.psum(partial_logits, 'pre')]
    all_gather x0 -> x1, waiting for transfers between devices: none -> 107 us  [error_rows(): logits = jnp.sum(lax.all_gather(partial_logits, 'pre'), axis=0)]
    reduce_sum x0 -> x1, other arithmetic: none -> 6.01 us  [error_rows(): logits = jnp.sum(lax.all_gather(partial_logits, 'pre'), axis=0)]
    all_gather x2, blocking collectives: 42.9 us -> 38.9 us  [prefix(): everything = jax.tree.map(lambda part: lax.all_gather(part, axis), value)]
where the time goes in v1:
time: 346 us; the launch traced here: 345 us
  waiting for transfers between devices  267 us (77%)
  blocking collectives  38.9 us (11%)
  between operations  13.8 us (4%)
  matrix products  12.8 us (4%)
  other arithmetic  10.6 us (3%)
    all_gather x1, waiting for transfers between devices, error_rows(): logits = jnp.sum(lax.all_gather(partial_logits, 'pre'), axis=0)  107 us
    all_gather x1, waiting for transfers between devices, shards(): signal_all = lax.all_gather(sources, 'pre', axis=0, tiled=True)  96 us
    all_gather x1, waiting for transfers between devices, shards(): lax.all_gather(traces, 'tm', axis=0, tiled=True)  42.7 us
    all_gather x2, blocking collectives, prefix(): everything = jax.tree.map(lambda part: lax.all_gather(part, axis), value)  38.9 us
    all_gather x1, waiting for transfers between devices, shards(): errors_all = lax.all_gather(errors, 'tm', axis=0, tiled=True)  21 us
    dot_general x1, matrix products, outer_sum(): lax.dot_general(left_rows, right_rows, (((0,), (0,)), ((), ())), preferre...  8.49 us
  transfers between devices with their start and end apart: 4, of which 4 were waited for; matrix products, arithmetic and copies ran while one was open for 2% of the time, Pallas kernels for 0%

profile of v1, /device:TPU:1, one launch (start us, length us, event | category | flops | bytes accessed | tf_op | source)
XLA Modules:
  0.0 345.3 jit_solution(13204293994232554518)
XLA Ops:
  6.5 0.0 copy-start
  6.5 0.0 copy-start.3
  6.5 0.0 all-gather.14.cloned.1.call-start
  6.5 2.3 fusion.3
  8.8 0.0 all-gather.14.cloned.1.call-update
  8.9 0.0 all-gather.10.cloned.1.call-start
  8.9 0.7 broadcast_subtract_fusion
  9.6 1.0 convert_multiply_fusion
  10.7 0.0 copy-start.1
  10.7 0.1 slice.194
  10.8 0.1 slice.192
  11.0 0.2 slice.190
  11.2 0.0 copy-done.3
  12.4 0.0 copy-done.1
  12.4 0.0 slice-start
  12.9 0.1 fusion.2
  13.0 0.2 slice-done
  13.2 0.1 pad.98
  13.2 0.1 pad.99
  13.3 20.9 %all-gather.1 = f32[16,1,512]{2,1,0:T(1,128)S(1)} all-gather(f32[1,1,512]{2,1,0:T(1,128)S(1)} %add_bitcast_fusion.1), channel_id=1, replica_groups=mesh['tm'=16,'pre'=32] {'tm'}, dimensions={0}, use_global_device_ids=true | all-gather | bytes 34816 | tf_op jit(solution)/shard_map/all_gather | solution.py:9
  34.2 0.1 pad.113
  34.3 0.1 pad.112
  34.4 107.1 %all-gather.14.cloned.1.call-done = f32[6144,512]{1,0:T(8,128)} async-done(((f32[192,512]{1,0:T(8,128)}), f32[6144,512]{1,0:T(8,128)}) %all-gather.14.cloned.1.call-update) | async-done | bytes 12582928 | tf_op jit(solution)/shard_map/all_gather | solution.py:38
  141.4 0.0 copy-start.4
  141.4 6.0 %reduce_sum.18 = f32[192,512]{1,0:T(8,128)S(1)} reduce(f32[32,192,512]{2,1,0:T(8,128)} %bitcast.30, f32[]{:T(128)} %constant.37.clone.1), dimensions={0}, to_apply=%region_2.0 | reduce | flops 3047424 | bytes 12976132 | tf_op jit(solution)/shard_map/reduce_sum | solution.py:38
  147.5 0.0 copy-start.2
  147.5 0.1 reduce_max.9
  147.6 0.2 fusion.1
  147.8 0.0 copy-done.4
  147.8 0.9 subtract_convert_fusion
  148.7 0.0 all-gather.10.cloned.1.call-update
  148.7 0.0 all-gather.8.cloned.1.call-start
  148.8 17.9 %all-gather.2 = f32[16,1,512]{2,1,0:T(1,128)S(1)} all-gather(f32[1,1,512]{2,1,0:T(1,128)S(1)} %add_bitcast_fusion), channel_id=1, replica_groups=mesh['tm'=16,'pre'=32] {'tm'}, dimensions={0}, use_global_device_ids=true | all-gather | bytes 34816 | tf_op jit(solution)/shard_map/all_gather | solution.py:9
  166.7 0.9 while.14
  167.6 0.8 add_convert_fusion
  168.4 0.0 all-gather.8.cloned.1.call-update
  168.5 0.0 all-gather.12.cloned.1.call-start
  168.5 21.0 %all-gather.10.cloned.1.call-done = bf16[3072,512]{1,0:T(8,128)(2,1)} async-done(((bf16[192,512]{1,0:T(8,128)(2,1)}), bf16[3072,512]{1,0:T(8,128)(2,1)}) %all-gather.10.cloned.1.call-update) | async-done | bytes 3145744 | tf_op jit(solution)/shard_map/all_gather | solution.py:61
  189.5 0.0 copy-done
  189.5 0.0 copy-done.2
  189.5 2.0 fusion
  191.6 0.0 all-gather.12.cloned.1.call-update
  191.6 42.7 %all-gather.8.cloned.1.call-done = bf16[3072,512]{1,0:T(8,128)(2,1)} async-done(((bf16[192,512]{1,0:T(8,128)(2,1)}), bf16[3072,512]{1,0:T(8,128)(2,1)}) %all-gather.8.cloned.1.call-update) | async-done | bytes 3145744 | tf_op jit(solution)/shard_map/all_gather | solution.py:74
  234.3 96.0 %all-gather.12.cloned.1.call-done = bf16[3072,1024]{1,0:T(8,128)(2,1)} async-done(((bf16[96,1024]{1,0:T(8,128)(2,1)}), bf16[3072,1024]{1,0:T(8,128)(2,1)}) %all-gather.12.cloned.1.call-update) | async-done | bytes 6291472 | tf_op jit(solution)/shard_map/all_gather | solution.py:73
  330.3 8.5 %fusion.19 = f32[512,1024]{1,0:T(8,128)} fusion(bf16[3072,512]{1,0:T(8,128)(2,1)} %all-gather.8.cloned.1.call-done, bf16[3072,1024]{1,0:T(8,128)(2,1)} %all-gather.12.cloned.1.call-done), kind=kOutput, calls=%fused_computation.73 | convolution fusion | flops 3221225472 | bytes 11534336 | tf_op jit(solution)/shard_map/dot_general | solution.py:54
  (116 shorter events, 1.6 us)
Async XLA Ops:
  6.5 183.0 %copy-start = (bf16[1024,512]{1,0:T(8,128)(2,1)S(1)}, bf16[1024,512]{1,0:T(8,128)(2,1)}, u32[]{:S(2)}) copy-start(bf16[1024,512]{1,0:T(8,128)(2,1)} %param.12) | copy-start | bytes 3145732
  6.5 4.7 %copy-start.3 = (f32[512]{0:T(512)S(1)}, f32[512]{0:T(512)}, u32[]{:S(2)}) copy-start(f32[512]{0:T(512)} %param.9) | copy-start | bytes 6148
  6.5 134.9 %all-gather.14.cloned.1.call-start = ((), (), s32[]{:S(2)}) async-start(), calls=%async_computation.3 | async-start | bytes 12976128 | tf_op jit(solution)/shard_map/all_gather | solution.py:38
  8.9 180.7 %all-gather.10.cloned.1.call-start = ((), (), s32[]{:S(2)}) async-start(), calls=%async_computation.1 | async-start | bytes 3342336 | tf_op jit(solution)/shard_map/all_gather | solution.py:61
  10.7 1.7 copy-start.1
  12.4 0.7 slice-start
  141.4 6.4 %copy-start.4 = (s32[192]{0:T(256)S(1)}, s32[192]{0:T(256)}, u32[]{:S(2)}) copy-start(s32[192]{0:T(256)} %param.13) | copy-start | bytes 2308
  147.5 42.1 %copy-start.2 = (bf16[96,1024]{1,0:T(8,128)(2,1)S(1)}, bf16[96,1024]{1,0:T(8,128)(2,1)}, u32[]{:S(2)}) copy-start(bf16[96,1024]{1,0:T(8,128)(2,1)} %param.10) | copy-start | bytes 589828
  148.7 85.6 %all-gather.8.cloned.1.call-start = ((), (), s32[]{:S(2)}) async-start(), calls=%async_computation | async-start | bytes 3342336 | tf_op jit(solution)/shard_map/all_gather | solution.py:74
  168.5 161.8 %all-gather.12.cloned.1.call-start = ((), (), s32[]{:S(2)}) async-start(), calls=%async_computation.2 | async-start | bytes 6488064 | tf_op jit(solution)/shard_map/all_gather | solution.py:73
Sparse Core Ops, SparseCore 0:
  10.5 130.8 all-gather.13
  148.8 40.6 all-gather.9
  191.7 42.6 all-gather.7
  237.3 92.9 all-gather.11

commit v2 on v0

--- a/solution.py
+++ b/solution.py
@@ -70,7 +70,9 @@
     traces = (states + powers * incoming[None, :]).astype(jnp.bfloat16)
     offset = lax.axis_index("pre") * pseudo_deriv.shape[0]
     sources = make_signal(errors_all, feedback_weight, pseudo_deriv, offset)
-    signal_all = lax.all_gather(sources, "pre", axis=0, tiled=True)
+    signal_all = jnp.concatenate(
+        lax.all_to_all(jnp.stack([sources] * lax.axis_size("pre")), "pre", 0, 0), axis=0
+    )
     return outer_sum(lax.all_gather(traces, "tm", axis=0, tiled=True), signal_all)
 
 

time: 375 us -> 393 us (1.048)
  waiting for transfers between devices: 295 us -> 312 us
  blocking collectives: 42.9 us -> 31 us
  starting transfers between devices: 0.13 us -> 10.2 us
    all_gather x1 -> x0, waiting for transfers between devices: 96.4 us -> none  [shards(): signal_all = lax.all_gather(sources, 'pre', axis=0, tiled=True)]
    all_to_all x0 -> x1, waiting for transfers between devices: none -> 65.8 us  [shards(): lax.all_to_all(jnp.stack([sources] * lax.axis_size('pre')), 'pre', 0, 0)]
    psum x1, waiting for transfers between devices: 134 us -> 160 us  [error_rows(): logits = lax.psum(partial_logits, 'pre')]
    all_gather x1, waiting for transfers between devices: 21.5 us -> 43.3 us  [shards(): errors_all = lax.all_gather(errors, 'tm', axis=0, tiled=True)]
    all_gather x2, blocking collectives: 42.9 us -> 31 us  [prefix(): everything = jax.tree.map(lambda part: lax.all_gather(part, axis), value)]
    all_to_all x0 -> x1, starting transfers between devices: none -> 10.1 us  [shards(): lax.all_to_all(jnp.stack([sources] * lax.axis_size('pre')), 'pre', 0, 0)]
  transfers between devices with their start and end apart: 4 -> 4, of which waited for: 4 -> 4; matrix products, arithmetic and copies ran while one was open for 2% -> 1% of each run, Pallas kernels for 0% -> 0%
where the time goes in v2:
time: 393 us; the launch traced here: 391 us
  waiting for transfers between devices  312 us (79%)
  blocking collectives  31 us (8%)
  between operations  13.8 us (4%)
  matrix products  12.1 us (3%)
  starting transfers between devices  10.2 us (3%)
  other arithmetic  5.93 us (2%)
  local copies, waits for them, and re-layouts  5.03 us (1%)
    psum x1, waiting for transfers between devices, error_rows(): logits = lax.psum(partial_logits, 'pre')  160 us
    all_to_all x1, waiting for transfers between devices, shards(): lax.all_to_all(jnp.stack([sources] * lax.axis_size('pre')), 'pre', 0, 0)  65.8 us
    all_gather x1, waiting for transfers between devices, shards(): errors_all = lax.all_gather(errors, 'tm', axis=0, tiled=True)  43.3 us
    all_gather x1, waiting for transfers between devices, shards(): lax.all_gather(traces, 'tm', axis=0, tiled=True)  43 us
    all_gather x2, blocking collectives, prefix(): everything = jax.tree.map(lambda part: lax.all_gather(part, axis), value)  31 us
    all_to_all x1, starting transfers between devices, shards(): lax.all_to_all(jnp.stack([sources] * lax.axis_size('pre')), 'pre', 0, 0)  10.1 us
    dot_general x1, matrix products, outer_sum(): lax.dot_general(left_rows, right_rows, (((0,), (0,)), ((), ())), preferre...  8.49 us
  transfers between devices with their start and end apart: 4, of which 4 were waited for; matrix products, arithmetic and copies ran while one was open for 1% of the time, Pallas kernels for 0%

profile of v2, /device:TPU:1, one launch (start us, length us, event | category | flops | bytes accessed | tf_op | source)
XLA Modules:
  0.0 390.6 jit_solution(6858952173470182282)
XLA Ops:
  6.5 0.0 copy-start
  6.5 0.0 copy-start.2
  6.5 0.0 copy-start.4
  6.5 0.0 all-reduce.30.cloned.1.call-start
  6.5 2.3 fusion.3
  8.8 0.0 all-reduce.30.cloned.1.call-update
  8.9 0.0 all-gather.7.cloned.1.call-start
  8.9 159.9 %all-reduce.30.cloned.1.call-done = f32[192,512]{1,0:T(8,128)} async-done(((f32[192,512]{1,0:T(8,128)}), f32[192,512]{1,0:T(8,128)}) %all-reduce.30.cloned.1.call-update) | async-done | bytes 393232 | tf_op jit(solution)/shard_map/psum | solution.py:38
  168.8 1.1 reduce_max.9
  169.9 1.2 fusion.1
  171.1 1.9 subtract_convert_fusion
  173.0 0.0 all-gather.7.cloned.1.call-update
  173.0 0.0 copy-done.4
  173.0 0.0 copy-done.2
  173.1 0.0 copy-start.1
  173.1 0.1 slice.194
  173.2 0.1 slice.192
  173.4 0.2 slice.190
  174.6 0.0 copy-start.3
  174.8 0.0 copy-done.1
  175.2 0.1 fusion.2
  175.3 43.3 %all-gather.7.cloned.1.call-done = bf16[3072,512]{1,0:T(8,128)(2,1)} async-done(((bf16[192,512]{1,0:T(8,128)(2,1)}), bf16[3072,512]{1,0:T(8,128)(2,1)}) %all-gather.7.cloned.1.call-update) | async-done | bytes 3145744 | tf_op jit(solution)/shard_map/all_gather | solution.py:61
  218.6 0.0 copy-done
  218.6 0.0 copy-done.3
  218.6 1.3 fusion
  220.0 3.4 stack.2
  223.4 0.0 slice-start
  223.4 10.1 %all-to-all-start = ((bf16[32,96,1024]{2,1,0:T(8,128)(2,1)}), bf16[32,96,1024]{2,1,0:T(8,128)(2,1)}, u32[]{:S(2)}, u32[]{:S(2)}) async-start(bf16[32,96,1024]{2,1,0:T(8,128)(2,1)} %stack.2), calls=%async_computation | async-start | bytes 12582912 | tf_op jit(solution)/shard_map/all_to_all | solution.py:74
  233.5 0.0 all-gather.5.cloned.1.call-start
  233.6 0.0 slice-done
  233.7 0.1 pad.98
  233.8 0.1 pad.99
  233.8 16.4 %all-gather = f32[16,1,512]{2,1,0:T(1,128)S(1)} all-gather(f32[1,1,512]{2,1,0:T(1,128)S(1)} %add_bitcast_fusion.1), channel_id=1, replica_groups=mesh['tm'=16,'pre'=32] {'tm'}, dimensions={0}, use_global_device_ids=true | all-gather | bytes 34816 | tf_op jit(solution)/shard_map/all_gather | solution.py:9
  250.3 0.1 pad.113
  250.4 0.1 pad.112
  250.4 14.5 %all-gather.1 = f32[16,1,512]{2,1,0:T(1,128)S(1)} all-gather(f32[1,1,512]{2,1,0:T(1,128)S(1)} %add_bitcast_fusion), channel_id=1, replica_groups=mesh['tm'=16,'pre'=32] {'tm'}, dimensions={0}, use_global_device_ids=true | all-gather | bytes 34816 | tf_op jit(solution)/shard_map/all_gather | solution.py:9
  265.0 0.9 while.14
  265.9 0.8 add_convert_fusion
  266.7 0.0 all-gather.5.cloned.1.call-update
  266.8 43.0 %all-gather.5.cloned.1.call-done = bf16[3072,512]{1,0:T(8,128)(2,1)} async-done(((bf16[192,512]{1,0:T(8,128)(2,1)}), bf16[3072,512]{1,0:T(8,128)(2,1)}) %all-gather.5.cloned.1.call-update) | async-done | bytes 3145744 | tf_op jit(solution)/shard_map/all_gather | solution.py:76
  309.8 65.8 %all-to-all-done = bf16[32,96,1024]{2,1,0:T(8,128)(2,1)} async-done(((bf16[32,96,1024]{2,1,0:T(8,128)(2,1)}), bf16[32,96,1024]{2,1,0:T(8,128)(2,1)}, u32[]{:S(2)}, u32[]{:S(2)}) %all-to-all-start) | async-done | bytes 6291488 | tf_op jit(solution)/shard_map/all_to_all | solution.py:74
  375.6 8.5 %fusion.19 = f32[512,1024]{1,0:T(8,128)} fusion(bf16[3072,512]{1,0:T(8,128)(2,1)} %all-gather.5.cloned.1.call-done, bf16[3072,1024]{1,0:T(8,128)(2,1)} %bitcast.11), kind=kOutput, calls=%fused_computation.73 | convolution fusion | flops 3221225472 | bytes 11534336 | tf_op jit(solution)/shard_map/dot_general | solution.py:54
  (118 shorter events, 1.7 us)
Async XLA Ops:
  6.5 212.1 %copy-start = (bf16[1024,512]{1,0:T(8,128)(2,1)S(1)}, bf16[1024,512]{1,0:T(8,128)(2,1)}, u32[]{:S(2)}) copy-start(bf16[1024,512]{1,0:T(8,128)(2,1)} %param.12) | copy-start | bytes 3145732
  6.5 166.5 %copy-start.2 = (s32[192,512]{1,0:T(8,128)S(1)}, s32[192,512]{1,0:T(8,128)}, u32[]{:S(2)}) copy-start(s32[192,512]{1,0:T(8,128)} %param.8) | copy-start | bytes 1179652
  6.5 166.5 %copy-start.4 = (f32[512]{0:T(512)S(1)}, f32[512]{0:T(512)}, u32[]{:S(2)}) copy-start(f32[512]{0:T(512)} %param.9) | copy-start | bytes 6148
  6.5 162.3 %all-reduce.30.cloned.1.call-start = ((), (), s32[]{:S(2)}) async-start(), calls=%async_computation.2 | async-start | bytes 786432 | tf_op jit(solution)/shard_map/psum | solution.py:38
  8.9 209.7 %all-gather.7.cloned.1.call-start = ((), (), s32[]{:S(2)}) async-start(), calls=%async_computation.3 | async-start | bytes 3342336 | tf_op jit(solution)/shard_map/all_gather | solution.py:61
  173.1 1.8 copy-start.1
  174.6 44.0 %copy-start.3 = (bf16[96,1024]{1,0:T(8,128)(2,1)S(1)}, bf16[96,1024]{1,0:T(8,128)(2,1)}, u32[]{:S(2)}) copy-start(bf16[96,1024]{1,0:T(8,128)(2,1)} %param.10) | copy-start | bytes 589828
  223.4 10.2 %slice-start = ((f32[192,512]{1,0:T(8,128)}), f32[1,512]{1,0:T(1,128)S(1)}, s32[]{:S(2)}) async-start(f32[192,512]{1,0:T(8,128)} %copy-done.1), calls=%async_computation.4 | async-start | bytes 4096 | tf_op jit(solution)/shard_map/slice | solution.py:31
  223.4 152.2 %all-to-all-start = ((bf16[32,96,1024]{2,1,0:T(8,128)(2,1)}), bf16[32,96,1024]{2,1,0:T(8,128)(2,1)}, u32[]{:S(2)}, u32[]{:S(2)}) async-start(bf16[32,96,1024]{2,1,0:T(8,128)(2,1)} %stack.2), calls=%async_computation | async-start | bytes 12582912 | tf_op jit(solution)/shard_map/all_to_all | solution.py:74
  233.5 76.3 %all-gather.5.cloned.1.call-start = ((), (), s32[]{:S(2)}) async-start(), calls=%async_computation.1 | async-start | bytes 3342336 | tf_op jit(solution)/shard_map/all_gather | solution.py:76
Sparse Core Ops, SparseCore 0:
  10.8 157.9 all-reduce.29
  173.1 45.4 all-gather.6
  266.9 42.8 all-gather.4
